TPU v7x, 32 devices: a whole 2x2x4 slice. The times are simulated.
32 devices in a mesh: gz: 2 (over x), gy: 4 (over z), gx: 4 (over y, core).
Axes of the slice: x: 2, y: 2, z: 4, core: 2. Of those that a mesh axis runs over, the one named last changes fastest.
Arguments:
- earlier_window_curl_state: float32 [2, 16, 512, 512], P(None, 'gz', 'gy', 'gx'), may hold values from -6 to 6
- material_resistivity_inverse: float32 [16, 512, 512], P('gz', 'gy', 'gx'), may hold values from 0.5 to 5
- winding_current_pattern: float32 [2, 512, 512], P(None, 'gy', 'gx'), may hold values from -8 to 8
- winding_axial_centre: int32 [1], replicated, may hold values from 0 to 15
- specimen_presence_flags: int32 [2, 64, 64], replicated, may hold values 0 or 1
- specimen_kelvin_values: float32 [16, 512, 384], P('gz', 'gy'), may hold values from -4 to 4
Outputs:
- potential_out: float32 [2, 16, 512, 512], P(None, 'gz', 'gy', 'gx')
- temperature_out: float32 [16, 512, 384], P('gz', 'gy')
All inputs are finite; a program needn't handle non-finite values.
Results may differ from a plain program's by a relative error of at most 0.00002.
Values sent between devices are 32-bit elements; how exact they have to be, the bound alone decides.
No kernel may reach another device: no remote copies, remote signals or barrier semaphores. Data moves between devices by JAX's collectives and lax.ppermute only.
A program may use at most 128 MiB of HBM per device.

v0:
```python
import jax
import jax.numpy as jnp
from jax import lax
from jax.sharding import PartitionSpec as P

MB = 8
STEPS = 4
WEIGHTS = (0.8, 1.0, 1.25)
SHIFT = 0.2
HEATING = 0.02
CONDUCT = 0.16
SOFTEN = 0.25


def padded(value, sides, width):
    for axis, dim in sides:
        peers, length = (lax.axis_size(axis), value.shape[dim])
        up = [(i, (i + 1) % peers) for i in range(peers - 1)]
        down = [(j, i) for i, j in up]
        last = lax.slice_in_dim(value, length - width, length, axis=dim)
        first = lax.slice_in_dim(value, 0, width, axis=dim)
        before = lax.ppermute(last, axis, up)
        after = lax.ppermute(first, axis, down)
        value = jnp.concatenate([before, value, after], axis=dim)
    return value


def expand_blocks(blocks):
    cells = jnp.repeat(blocks, MB, axis=0)
    cells = jnp.repeat(cells, MB, axis=1)
    return jnp.repeat(cells, MB, axis=2).astype(jnp.float32)


def neighbours(bordered_segment):
    total = bordered_segment[:, 2:, 1:-1, 1:-1] + bordered_segment[:, :-2, 1:-1, 1:-1]
    total = total + bordered_segment[:, 1:-1, 2:, 1:-1] + bordered_segment[:, 1:-1, :-2, 1:-1]
    return total + bordered_segment[:, 1:-1, 1:-1, 2:] + bordered_segment[:, 1:-1, 1:-1, :-2]


def relax(magnetic_curl_state, beside, source, coupling, factor):
    diagonal = 6.0 + SHIFT
    real_res = source[0] - (
        diagonal * magnetic_curl_state[0] - coupling * magnetic_curl_state[1] - beside[0]
    )
    imag_res = source[1] - (
        diagonal * magnetic_curl_state[1] + coupling * magnetic_curl_state[0] - beside[1]
    )
    scaled = factor / (diagonal * diagonal + coupling * coupling)
    return jnp.stack(
        [
            magnetic_curl_state[0] + scaled * (diagonal * real_res + coupling * imag_res),
            magnetic_curl_state[1] + scaled * (diagonal * imag_res - coupling * real_res),
        ]
    )


def six_faces(array):
    return [
        array[2:, 1:-1, 1:-1],
        array[:-2, 1:-1, 1:-1],
        array[1:-1, 2:, 1:-1],
        array[1:-1, :-2, 1:-1],
        array[1:-1, 1:-1, 2:],
        array[1:-1, 1:-1, :-2],
    ]


def diffusivity_coefficient(bordered_segment, bordered_segment_flags, ohmic_dissipation):
    centre = bordered_segment[1:-1, 1:-1, 1:-1]
    centre_mask = bordered_segment_flags[1:-1, 1:-1, 1:-1]
    centre_kappa = 1.0 / (1.0 + SOFTEN * centre * centre)
    flux = jnp.zeros_like(centre)
    for other, other_mask in zip(six_faces(bordered_segment), six_faces(bordered_segment_flags)):
        kappa = 1.0 / (1.0 + SOFTEN * other * other)
        flux = flux + other_mask * (centre_kappa + kappa) * (other - centre)
    return centre + 0.5 * CONDUCT * centre_mask * flux + ohmic_dissipation


def thermal_mask(
    specimen_presence_flags, z_start, row_start, depth, rows, specimen_column_sum, column_offset
):
    window = jnp.pad(specimen_presence_flags[:, :, column_offset // MB :], 1)
    blocks = lax.dynamic_slice(
        window,
        (z_start // MB, row_start // MB, 0),
        (depth // MB + 2, rows // MB + 2, window.shape[2]),
    )
    cells = expand_blocks(blocks)
    return cells[
        MB - 1 : MB + 1 + depth, MB - 1 : MB + 1 + rows, MB - 1 : MB + 1 + specimen_column_sum
    ]


def coil_profile(first, count, winding_axial_centre, coil_width):
    axial = (
        (first + jnp.arange(count)).astype(jnp.float32)
        - winding_axial_centre[0].astype(jnp.float32)
    ) / coil_width
    return 1.0 / (1.0 + axial * axial)


def on_device(
    earlier_window_curl_state,
    material_resistivity_inverse,
    winding_current_pattern,
    winding_axial_centre,
    specimen_presence_flags,
    specimen_kelvin_values,
):
    depth, height, breadth = material_resistivity_inverse.shape
    z_total = depth * lax.axis_size("gz")
    x_total = breadth * lax.axis_size("gx")
    z_start = lax.axis_index("gz") * depth
    y_start = lax.axis_index("gy") * height
    x_start = lax.axis_index("gx") * breadth
    own_blocks = lax.dynamic_slice(
        specimen_presence_flags,
        (z_start // MB, y_start // MB, x_start // MB),
        (depth // MB, height // MB, breadth // MB),
    )
    coupling = expand_blocks(own_blocks) * material_resistivity_inverse
    coil_width = z_total // 4
    magnetic_curl_state = earlier_window_curl_state
    profile = coil_profile(z_start, depth, winding_axial_centre, coil_width)
    source = profile[None, :, None, None] * winding_current_pattern[:, None, :, :]
    for factor in WEIGHTS:
        bordered_segment = padded(magnetic_curl_state, (("gz", 1), ("gy", 2), ("gx", 3)), 1)
        magnetic_curl_state = relax(
            magnetic_curl_state, neighbours(bordered_segment), source, coupling, factor
        )
    ohmic_dissipation = (
        HEATING
        * coupling
        * (
            magnetic_curl_state[0] * magnetic_curl_state[0]
            + magnetic_curl_state[1] * magnetic_curl_state[1]
        )
    )
    specimen_column_sum = specimen_kelvin_values.shape[2]
    column_offset = x_total - specimen_column_sum
    rows = height // lax.axis_size("gx")
    moved = lax.all_to_all(ohmic_dissipation, "gx", split_axis=1, concat_axis=2, tiled=True)
    block_heat_source = moved[:, :, column_offset:]
    row_start = y_start + lax.axis_index("gx") * rows
    segment_kelvin = lax.dynamic_slice_in_dim(
        specimen_kelvin_values, lax.axis_index("gx") * rows, rows, 1
    )
    bordered_segment_flags = thermal_mask(
        specimen_presence_flags, z_start, row_start, depth, rows, specimen_column_sum, column_offset
    )
    for number in range(STEPS):
        bordered_segment = padded(segment_kelvin, (("gz", 0), (("gy", "gx"), 1)), 1)
        segment_kelvin = diffusivity_coefficient(
            jnp.pad(bordered_segment, ((0, 0), (0, 0), (1, 1))),
            bordered_segment_flags,
            block_heat_source,
        )
    segment_kelvin = lax.all_gather(segment_kelvin, "gx", axis=1, tiled=True)
    return (magnetic_curl_state, segment_kelvin)


def solution(mesh):
    placed = (
        P(None, "gz", "gy", "gx"),
        P("gz", "gy", "gx"),
        P(None, "gy", "gx"),
        P(),
        P(),
        P("gz", "gy", None),
    )
    return jax.shard_map(
        on_device,
        mesh=mesh,
        in_specs=placed,
        out_specs=(P(None, "gz", "gy", "gx"), P("gz", "gy", None)),
        check_vma=False,
    )
```

profile of v0, /device:TPU:0, one launch (start us, length us, event | category | flops | bytes accessed | tf_op | source)
XLA Modules:
  0.0 264.0 jit_solution(12692609611169328279)
XLA Ops:
  7.2 2.1 copy.246
  9.9 5.0 %collective-permute-start.1 = (f32[2,1,128,128]{3,0,2,1:T(2,128)S(1)}, f32[2,1,128,128]{3,0,2,1:T(2,128)S(1)}, u32[]{:S(2)}, u32[]{:S(2)}) collective-permute-start(f32[2,1,128,128]{3,0,2,1:T(2,128)S(1)} %get-tuple-element.49), channel_id=1, source_target_pairs={{0,16},{1,17},{2,18},{3,19},{4,20},{5,21},{6,22},{7,23},{8,24},{9,... | collective-permute-start | bytes 393224 | tf_op jit(solution)/shard_map/ppermute | solution.py:22
  18.8 3.3 %collective-permute-done = f32[2,1,128,128]{3,0,2,1:T(2,128)} collective-permute-done((f32[2,1,128,128]{3,0,2,1:T(2,128)}, f32[2,1,128,128]{3,0,2,1:T(2,128)}, u32[]{:S(2)}, u32[]{:S(2)}) %collective-permute-start) | collective-permute-done | bytes 131104 | tf_op jit(solution)/shard_map/ppermute | solution.py:23
  24.9 5.1 %collective-permute-start.3 = (f32[2,10,1,128]{3,0,2,1:T(2,128)}, f32[2,10,1,128]{3,0,2,1:T(2,128)}, u32[]{:S(2)}, u32[]{:S(2)}) collective-permute-start(f32[2,10,1,128]{3,0,2,1:T(2,128)} %get-tuple-element.40), channel_id=1, source_target_pairs={{0,4},{4,8},{8,12},{1,5},{5,9},{9,13},{2,6},{6,10},{10,14},{3,7},{... | collective-permute-start | bytes 30728 | tf_op jit(solution)/shard_map/ppermute | solution.py:22
  33.6 3.0 %fusion.213 = (f32[2,10,130,1]{3,0,2,1:T(2,128)}, f32[2,10,130,1]{3,0,2,1:T(2,128)}) fusion(f32[2,10,130,128]{3,0,2,1:T(2,128)S(1)} %pad_maximum_fusion.2), kind=kLoop, calls=%fused_computation.410 | loop fusion | bytes 41600 | tf_op jit(solution)/shard_map/slice | solution.py:21
  36.5 2.5 copy.250
  40.3 2.5 copy.252
  42.9 3.6 %collective-permute-start.5 = (f32[2,10,130,1]{2,0,3,1:T(2,128)}, f32[2,10,130,1]{2,0,3,1:T(2,128)}, u32[]{:S(2)}, u32[]{:S(2)}) collective-permute-start(f32[2,10,130,1]{2,0,3,1:T(2,128)} %copy.252), channel_id=1, source_target_pairs={{0,1},{1,2},{2,3},{4,5},{5,6},{6,7},{8,9},{9,10},{10,11},{12,13},{... | collective-permute-start | bytes 31208 | tf_op jit(solution)/shard_map/ppermute | solution.py:22
  46.6 2.4 copy.251
  49.1 2.4 copy.253
  51.5 7.2 %fusion.10 = f32[2,8,128,128]{3,0,2,1:T(2,128)S(1)} fusion(f32[2,10,130,1]{3,0,2,1:T(2,128)} %copy.253, f32[2,10,1,128]{3,0,2,1:T(2,128)S(1)} %collective-permute-done.2, f32[2,10,128,128]{3,0,2,1:T(2,128)S(1)} %constant_dynamic-update-slice_fusion, f32[2,10,1,128]{3,0,2,1:T(2,128)} %collective-permute-done.3, f32[2,10,130,1]{3,0,2,1:T(2,128)} %copy.251, ...), kind=kLoop, calls=%fused_computation.65 | loop fusion | flops 3932160 | bytes 3711296 | tf_op jit(solution)/shard_map/add | solution.py:37
  61.5 4.6 %collective-permute-start.7 = (f32[2,1,128,128]{3,2,1,0:T(8,128)S(1)}, f32[2,1,128,128]{3,2,1,0:T(8,128)S(1)}, u32[]{:S(2)}, u32[]{:S(2)}) collective-permute-start(f32[2,1,128,128]{3,2,1,0:T(8,128)S(1)} %get-tuple-element.44), channel_id=1, source_target_pairs={{0,16},{1,17},{2,18},{3,19},{4,20},{5,21},{6,22},{7,23},{8,24},{9,... | collective-permute-start | bytes 393224 | tf_op jit(solution)/shard_map/ppermute | solution.py:22
  68.8 5.2 %collective-permute-start.19 = (f32[1,32,384]{2,1,0:T(8,128)}, f32[1,32,384]{2,1,0:T(8,128)}, u32[]{:S(2)}, u32[]{:S(2)}) collective-permute-start(f32[1,32,384]{2,1,0:T(8,128)} %get-tuple-element.28), channel_id=1, source_target_pairs={{0,16},{1,17},{2,18},{3,19},{4,20},{5,21},{6,22},{7,23},{8,24},{9,... | collective-permute-start | bytes 147464 | tf_op jit(solution)/shard_map/ppermute | solution.py:22
  75.4 4.5 %collective-permute-start.9 = (f32[2,10,1,128]{3,0,2,1:T(2,128)S(1)}, f32[2,10,1,128]{3,0,2,1:T(2,128)S(1)}, u32[]{:S(2)}, u32[]{:S(2)}) collective-permute-start(f32[2,10,1,128]{3,0,2,1:T(2,128)S(1)} %copy.257), channel_id=1, source_target_pairs={{0,4},{4,8},{8,12},{1,5},{5,9},{9,13},{2,6},{6,10},{10,14},{3,7},{... | collective-permute-start | bytes 30728 | tf_op jit(solution)/shard_map/ppermute | solution.py:22
  81.5 2.0 fusion.212
  83.5 2.1 copy.261
  86.9 2.1 copy.263
  89.0 3.2 %collective-permute-start.11 = (f32[2,10,130,1]{2,0,3,1:T(2,128)S(1)}, f32[2,10,130,1]{2,0,3,1:T(2,128)S(1)}, u32[]{:S(2)}, u32[]{:S(2)}) collective-permute-start(f32[2,10,130,1]{2,0,3,1:T(2,128)S(1)} %copy.263), channel_id=1, source_target_pairs={{0,1},{1,2},{2,3},{4,5},{5,6},{6,7},{8,9},{9,10},{10,11},{12,13},{... | collective-permute-start | bytes 31208 | tf_op jit(solution)/shard_map/ppermute | solution.py:22
  93.4 1.6 copy.262
  96.7 3.4 %fusion.5 = f32[2,8,128,128]{3,2,1,0:T(8,128)S(1)} fusion(f32[2,10,130,1]{3,2,1,0:T(8,128)} %copy.264, f32[2,10,1,128]{3,2,1,0:T(1,128)S(1)} %copy.256, f32[2,10,1,128]{3,2,1,0:T(1,128)S(1)} %copy.258, f32[2,1,128,128]{3,2,1,0:T(8,128)S(1)} %collective-permute-done.6, f32[2,1,128,128]{3,2,1,0:T(8,128)S(1)} %collective-permute-done.7, ...), kind=kLoop, calls=%fused_computation.36 | loop fusion | flops 7602176 | bytes 2400576 | tf_op jit(solution)/shard_map/add | solution.py:37
  102.0 4.6 %collective-permute-start.13 = (f32[2,1,128,128]{3,2,1,0:T(8,128)S(1)}, f32[2,1,128,128]{3,2,1,0:T(8,128)S(1)}, u32[]{:S(2)}, u32[]{:S(2)}) collective-permute-start(f32[2,1,128,128]{3,2,1,0:T(8,128)S(1)} %get-tuple-element.42), channel_id=1, source_target_pairs={{0,16},{1,17},{2,18},{3,19},{4,20},{5,21},{6,22},{7,23},{8,24},{9,... | collective-permute-start | bytes 393224 | tf_op jit(solution)/shard_map/ppermute | solution.py:22
  106.5 2.5 broadcast_bitcast_fusion
  111.6 4.8 %collective-permute-start.15 = (f32[2,10,1,128]{3,0,2,1:T(2,128)S(1)}, f32[2,10,1,128]{3,0,2,1:T(2,128)S(1)}, u32[]{:S(2)}, u32[]{:S(2)}) collective-permute-start(f32[2,10,1,128]{3,0,2,1:T(2,128)S(1)} %copy.267), channel_id=1, source_target_pairs={{0,4},{4,8},{8,12},{1,5},{5,9},{9,13},{2,6},{6,10},{10,14},{3,7},{... | collective-permute-start | bytes 30728 | tf_op jit(solution)/shard_map/ppermute | solution.py:22
  118.0 2.0 fusion.211
  120.0 2.1 copy.271
  123.4 2.1 copy.273
  125.5 3.0 %collective-permute-start.17 = (f32[2,10,130,1]{2,0,3,1:T(2,128)S(1)}, f32[2,10,130,1]{2,0,3,1:T(2,128)S(1)}, u32[]{:S(2)}, u32[]{:S(2)}) collective-permute-start(f32[2,10,130,1]{2,0,3,1:T(2,128)S(1)} %copy.273), channel_id=1, source_target_pairs={{0,1},{1,2},{2,3},{4,5},{5,6},{6,7},{8,9},{9,10},{10,11},{12,13},{... | collective-permute-start | bytes 31208 | tf_op jit(solution)/shard_map/ppermute | solution.py:22
  131.2 3.2 %collective-permute-start.21 = (f32[10,1,384]{2,1,0:T(1,128)}, f32[10,1,384]{2,1,0:T(1,128)S(1)}, u32[]{:S(2)}, u32[]{:S(2)}) collective-permute-start(f32[10,1,384]{2,1,0:T(1,128)} %get-tuple-element.57), channel_id=1, source_target_pairs={{0,1},{1,2},{2,3},{3,4},{4,5},{5,6},{6,7},{7,8},{8,9},{9,10},{10,1... | collective-permute-start | bytes 46088 | tf_op jit(solution)/shard_map/ppermute | solution.py:22
  137.7 3.4 %fusion = f32[2,8,128,128]{3,2,1,0:T(8,128)S(1)} fusion(f32[2,10,130,1]{3,2,1,0:T(8,128)} %copy.274, f32[2,10,1,128]{3,2,1,0:T(1,128)S(1)} %copy.266, f32[2,10,1,128]{3,2,1,0:T(1,128)S(1)} %copy.268, f32[2,1,128,128]{3,2,1,0:T(8,128)S(1)} %collective-permute-done.12, f32[2,1,128,128]{3,2,1,0:T(8,128)S(1)} %collective-permute-done.13, ...), kind=kLoop, calls=%fused_computation.7 | loop fusion | flops 7602176 | bytes 2400576 | tf_op jit(solution)/shard_map/add | solution.py:37
  143.7 4.1 %all-to-all-start = ((f32[8,128,128]{2,0,1:T(8,128)}), f32[8,128,128]{2,0,1:T(8,128)}, u32[]{:S(2)}, u32[]{:S(2)}) async-start(f32[8,128,128]{2,0,1:T(8,128)} %copy.283), calls=%async_computation | async-start | bytes 1048576 | tf_op jit(solution)/shard_map/all_to_all | solution.py:142
  148.1 12.0 %fusion.210 = (f32[8,32,384]{1,2,0:T(8,128)}, f32[8,32,384]{1,2,0:T(8,128)}, f32[8,32,384]{1,2,0:T(8,128)}, f32[8,32,384]{1,2,0:T(8,128)}, f32[8,32,384]{1,2,0:T...) fusion(f32[24,48,400]{1,2,0:T(8,128)} %broadcast_bitcast_fusion), kind=kLoop, calls=%fused_computation.407 | loop fusion | bytes 5505024 | tf_op jit(solution)/shard_map/slice | solution.py:70
  160.1 1.8 copy.288
  162.0 1.9 copy.289
  164.3 1.9 copy.291
  166.1 1.9 copy.292
  168.0 1.9 copy.293
  169.8 1.9 copy.294
  171.8 2.1 select_maximum_fusion.12
  173.8 2.2 copy.297
  177.3 3.0 %fusion.47 = f32[8,32,384]{2,1,0:T(8,128)S(1)} fusion(f32[8,32,384]{2,1,0:T(8,128)} %copy-done.1, f32[8,32,384]{2,1,0:T(8,128)S(1)} %copy.289, f32[8,32,384]{2,1,0:T(8,128)S(1)} %copy.290, f32[8,32,384]{2,1,0:T(8,128)S(1)} %copy.291, f32[8,32,384]{2,1,0:T(8,128)S(1)} %copy.292, f32[8,32,384]{2,1,0:T(8,128)S(1)} %copy.293, f32[8,32,384]{2,1,0:T(8,128)S(1)} %copy.294, ...), kind=kLoop, calls=%fused_computation.176 | loop fusion | flops 6782976 | bytes 4847616 | tf_op jit(solution)/shard_map/add | solution.py:76
  181.6 4.5 %collective-permute-start.23 = (f32[1,32,384]{2,1,0:T(8,128)S(1)}, f32[1,32,384]{2,1,0:T(8,128)S(1)}, u32[]{:S(2)}, u32[]{:S(2)}) collective-permute-start(f32[1,32,384]{2,1,0:T(8,128)S(1)} %get-tuple-element.62), channel_id=1, source_target_pairs={{0,16},{1,17},{2,18},{3,19},{4,20},{5,21},{6,22},{7,23},{8,24},{9,... | collective-permute-start | bytes 147464 | tf_op jit(solution)/shard_map/ppermute | solution.py:22
  189.2 3.2 %collective-permute-start.25 = (f32[10,1,384]{2,1,0:T(1,128)S(1)}, f32[10,1,384]{2,1,0:T(1,128)S(1)}, u32[]{:S(2)}, u32[]{:S(2)}) collective-permute-start(f32[10,1,384]{2,1,0:T(1,128)S(1)} %get-tuple-element.55), channel_id=1, source_target_pairs={{0,1},{1,2},{2,3},{3,4},{4,5},{5,6},{6,7},{7,8},{8,9},{9,10},{10,1... | collective-permute-start | bytes 46088 | tf_op jit(solution)/shard_map/ppermute | solution.py:22
  195.9 4.5 %collective-permute-start.27 = (f32[1,32,384]{2,1,0:T(8,128)S(1)}, f32[1,32,384]{2,1,0:T(8,128)S(1)}, u32[]{:S(2)}, u32[]{:S(2)}) collective-permute-start(f32[1,32,384]{2,1,0:T(8,128)S(1)} %get-tuple-element.60), channel_id=1, source_target_pairs={{0,16},{1,17},{2,18},{3,19},{4,20},{5,21},{6,22},{7,23},{8,24},{9,... | collective-permute-start | bytes 147464 | tf_op jit(solution)/shard_map/ppermute | solution.py:22
  203.5 3.2 %collective-permute-start.29 = (f32[10,1,384]{2,1,0:T(1,128)S(1)}, f32[10,1,384]{2,1,0:T(1,128)S(1)}, u32[]{:S(2)}, u32[]{:S(2)}) collective-permute-start(f32[10,1,384]{2,1,0:T(1,128)S(1)} %get-tuple-element.53), channel_id=1, source_target_pairs={{0,1},{1,2},{2,3},{3,4},{4,5},{5,6},{6,7},{7,8},{8,9},{9,10},{10,1... | collective-permute-start | bytes 46088 | tf_op jit(solution)/shard_map/ppermute | solution.py:22
  210.1 4.5 %collective-permute-start.31 = (f32[1,32,384]{2,1,0:T(8,128)S(1)}, f32[1,32,384]{2,1,0:T(8,128)S(1)}, u32[]{:S(2)}, u32[]{:S(2)}) collective-permute-start(f32[1,32,384]{2,1,0:T(8,128)S(1)} %get-tuple-element.58), channel_id=1, source_target_pairs={{0,16},{1,17},{2,18},{3,19},{4,20},{5,21},{6,22},{7,23},{8,24},{9,... | collective-permute-start | bytes 147464 | tf_op jit(solution)/shard_map/ppermute | solution.py:22
  217.7 4.8 %collective-permute-start.33 = (f32[10,1,384]{2,1,0:T(1,128)S(1)}, f32[10,1,384]{2,1,0:T(1,128)S(1)}, u32[]{:S(2)}, u32[]{:S(2)}) collective-permute-start(f32[10,1,384]{2,1,0:T(1,128)S(1)} %get-tuple-element.51), channel_id=1, source_target_pairs={{0,1},{1,2},{2,3},{3,4},{4,5},{5,6},{6,7},{7,8},{8,9},{9,10},{10,1... | collective-permute-start | bytes 46088 | tf_op jit(solution)/shard_map/ppermute | solution.py:22
  227.0 27.3 %all-gather.2.cloned.1.call-done = f32[8,128,384]{2,0,1:T(8,128)} async-done(((f32[8,32,384]{2,0,1:T(8,128)}), f32[8,128,384]{2,0,1:T(8,128)}) %all-gather.2.cloned.1.call-update) | async-done | bytes 1572880 | tf_op jit(solution)/shard_map/all_gather | solution.py:158
  254.3 2.9 %copy.286 = f32[8,128,384]{2,1,0:T(8,128)} copy(f32[8,128,384]{2,0,1:T(8,128)} %all-gather.2.cloned.1.call-done) | data formatting | bytes 3145728
  (144 shorter events, 63.3 us)
Async XLA Ops:
  7.2 9.7 %copy-start.12 = (f32[2,128,128]{2,1,0:T(8,128)S(1)}, f32[2,128,128]{2,1,0:T(8,128)}, u32[]{:S(2)}) copy-start(f32[2,128,128]{2,1,0:T(8,128)} %param.8) | copy-start | bytes 393220
  9.2 7.6 %copy-start.2 = (f32[2,8,128,128]{3,0,2,1:T(2,128)}, f32[2,8,128,128]{3,0,2,1:T(2,128)S(1)}, u32[]{:S(2)}) copy-start(f32[2,8,128,128]{3,0,2,1:T(2,128)S(1)} %copy.246) | copy-start | bytes 3145732
  9.3 8.7 %copy-start = (f32[2,8,128,128]{3,2,1,0:T(8,128)S(1)}, f32[2,8,128,128]{3,2,1,0:T(8,128)}, u32[]{:S(2)}) copy-start(f32[2,8,128,128]{3,2,1,0:T(8,128)} %param.6) | copy-start | bytes 3145732
  9.9 8.0 %collective-permute-start.1 = (f32[2,1,128,128]{3,0,2,1:T(2,128)S(1)}, f32[2,1,128,128]{3,0,2,1:T(2,128)S(1)}, u32[]{:S(2)}, u32[]{:S(2)}) collective-permute-start(f32[2,1,128,128]{3,0,2,1:T(2,128)S(1)} %get-tuple-element.49), channel_id=1, source_target_pairs={{0,16},{1,17},{2,18},{3,19},{4,20},{5,21},{6,22},{7,23},{8,24},{9,... | collective-permute-start | bytes 393224 | tf_op jit(solution)/shard_map/ppermute | solution.py:22
  14.9 7.2 %collective-permute-start = (f32[2,1,128,128]{3,0,2,1:T(2,128)}, f32[2,1,128,128]{3,0,2,1:T(2,128)}, u32[]{:S(2)}, u32[]{:S(2)}) collective-permute-start(f32[2,1,128,128]{3,0,2,1:T(2,128)} %get-tuple-element.48), channel_id=1, source_target_pairs={{16,0},{17,1},{18,2},{19,3},{20,4},{21,5},{22,6},{23,7},{24,8},{25... | collective-permute-start | bytes 393224 | tf_op jit(solution)/shard_map/ppermute | solution.py:23
  17.9 14.3 %copy-start.9 = (f32[2,1,128,128]{3,0,2,1:T(2,128)}, f32[2,1,128,128]{3,0,2,1:T(2,128)S(1)}, u32[]{:S(2)}) copy-start(f32[2,1,128,128]{3,0,2,1:T(2,128)S(1)} %collective-permute-done.1) | copy-start | bytes 393220
  23.7 8.6 %collective-permute-start.2 = (f32[2,10,1,128]{3,0,2,1:T(2,128)}, f32[2,10,1,128]{3,0,2,1:T(2,128)S(1)}, u32[]{:S(2)}, u32[]{:S(2)}) collective-permute-start(f32[2,10,1,128]{3,0,2,1:T(2,128)} %get-tuple-element.41), channel_id=1, source_target_pairs={{4,0},{8,4},{12,8},{5,1},{9,5},{13,9},{6,2},{10,6},{14,10},{7,3},{... | collective-permute-start | bytes 30728 | tf_op jit(solution)/shard_map/ppermute | solution.py:23
  24.9 7.3 %collective-permute-start.3 = (f32[2,10,1,128]{3,0,2,1:T(2,128)}, f32[2,10,1,128]{3,0,2,1:T(2,128)}, u32[]{:S(2)}, u32[]{:S(2)}) collective-permute-start(f32[2,10,1,128]{3,0,2,1:T(2,128)} %get-tuple-element.40), channel_id=1, source_target_pairs={{0,4},{4,8},{8,12},{1,5},{5,9},{9,13},{2,6},{6,10},{10,14},{3,7},{... | collective-permute-start | bytes 30728 | tf_op jit(solution)/shard_map/ppermute | solution.py:22
  36.5 10.0 %copy-start.15 = (f32[128,16]{0,1:T(8,128)S(1)}, f32[128,16]{0,1:T(8,128)}, u32[]{:S(2)}) copy-start(f32[128,16]{0,1:T(8,128)} %copy.243) | copy-start | bytes 24580
  39.1 7.6 %collective-permute-start.4 = (f32[2,10,130,1]{2,0,3,1:T(2,128)}, f32[2,10,130,1]{2,0,3,1:T(2,128)}, u32[]{:S(2)}, u32[]{:S(2)}) collective-permute-start(f32[2,10,130,1]{2,0,3,1:T(2,128)} %copy.250), channel_id=1, source_target_pairs={{1,0},{2,1},{3,2},{5,4},{6,5},{7,6},{9,8},{10,9},{11,10},{13,12},{... | collective-permute-start | bytes 31208 | tf_op jit(solution)/shard_map/ppermute | solution.py:23
  42.9 6.2 %collective-permute-start.5 = (f32[2,10,130,1]{2,0,3,1:T(2,128)}, f32[2,10,130,1]{2,0,3,1:T(2,128)}, u32[]{:S(2)}, u32[]{:S(2)}) collective-permute-start(f32[2,10,130,1]{2,0,3,1:T(2,128)} %copy.252), channel_id=1, source_target_pairs={{0,1},{1,2},{2,3},{4,5},{5,6},{6,7},{8,9},{9,10},{10,11},{12,13},{... | collective-permute-start | bytes 31208 | tf_op jit(solution)/shard_map/ppermute | solution.py:22
  60.1 13.8 %copy-start.13 = (s32[2,64,64]{2,1,0:T(8,128)S(1)}, s32[2,64,64]{2,1,0:T(8,128)}, u32[]{:S(2)}) copy-start(s32[2,64,64]{2,1,0:T(8,128)} %param.10) | copy-start | bytes 98308
  60.2 13.9 %collective-permute-start.6 = (f32[2,1,128,128]{3,2,1,0:T(8,128)S(1)}, f32[2,1,128,128]{3,2,1,0:T(8,128)S(1)}, u32[]{:S(2)}, u32[]{:S(2)}) collective-permute-start(f32[2,1,128,128]{3,2,1,0:T(8,128)S(1)} %get-tuple-element.45), channel_id=1, source_target_pairs={{16,0},{17,1},{18,2},{19,3},{20,4},{21,5},{22,6},{23,7},{24,8},{25... | collective-permute-start | bytes 393224 | tf_op jit(solution)/shard_map/ppermute | solution.py:23
  61.5 12.6 %collective-permute-start.7 = (f32[2,1,128,128]{3,2,1,0:T(8,128)S(1)}, f32[2,1,128,128]{3,2,1,0:T(8,128)S(1)}, u32[]{:S(2)}, u32[]{:S(2)}) collective-permute-start(f32[2,1,128,128]{3,2,1,0:T(8,128)S(1)} %get-tuple-element.44), channel_id=1, source_target_pairs={{0,16},{1,17},{2,18},{3,19},{4,20},{5,21},{6,22},{7,23},{8,24},{9,... | collective-permute-start | bytes 393224 | tf_op jit(solution)/shard_map/ppermute | solution.py:22
  67.5 61.0 %collective-permute-start.18 = (f32[1,32,384]{2,1,0:T(8,128)}, f32[1,32,384]{2,1,0:T(8,128)S(1)}, u32[]{:S(2)}, u32[]{:S(2)}) collective-permute-start(f32[1,32,384]{2,1,0:T(8,128)} %get-tuple-element.29), channel_id=1, source_target_pairs={{16,0},{17,1},{18,2},{19,3},{20,4},{21,5},{22,6},{23,7},{24,8},{25... | collective-permute-start | bytes 147464 | tf_op jit(solution)/shard_map/ppermute | solution.py:23
  68.8 59.7 %collective-permute-start.19 = (f32[1,32,384]{2,1,0:T(8,128)}, f32[1,32,384]{2,1,0:T(8,128)}, u32[]{:S(2)}, u32[]{:S(2)}) collective-permute-start(f32[1,32,384]{2,1,0:T(8,128)} %get-tuple-element.28), channel_id=1, source_target_pairs={{0,16},{1,17},{2,18},{3,19},{4,20},{5,21},{6,22},{7,23},{8,24},{9,... | collective-permute-start | bytes 147464 | tf_op jit(solution)/shard_map/ppermute | solution.py:22
  74.1 6.0 %collective-permute-start.8 = (f32[2,10,1,128]{3,0,2,1:T(2,128)S(1)}, f32[2,10,1,128]{3,0,2,1:T(2,128)S(1)}, u32[]{:S(2)}, u32[]{:S(2)}) collective-permute-start(f32[2,10,1,128]{3,0,2,1:T(2,128)S(1)} %copy.255), channel_id=1, source_target_pairs={{4,0},{8,4},{12,8},{5,1},{9,5},{13,9},{6,2},{10,6},{14,10},{7,3},{... | collective-permute-start | bytes 30728 | tf_op jit(solution)/shard_map/ppermute | solution.py:23
  75.4 5.9 %collective-permute-start.9 = (f32[2,10,1,128]{3,0,2,1:T(2,128)S(1)}, f32[2,10,1,128]{3,0,2,1:T(2,128)S(1)}, u32[]{:S(2)}, u32[]{:S(2)}) collective-permute-start(f32[2,10,1,128]{3,0,2,1:T(2,128)S(1)} %copy.257), channel_id=1, source_target_pairs={{0,4},{4,8},{8,12},{1,5},{5,9},{9,13},{2,6},{6,10},{10,14},{3,7},{... | collective-permute-start | bytes 30728 | tf_op jit(solution)/shard_map/ppermute | solution.py:22
  85.6 7.8 %collective-permute-start.10 = (f32[2,10,130,1]{2,0,3,1:T(2,128)S(1)}, f32[2,10,130,1]{2,0,3,1:T(2,128)S(1)}, u32[]{:S(2)}, u32[]{:S(2)}) collective-permute-start(f32[2,10,130,1]{2,0,3,1:T(2,128)S(1)} %copy.261), channel_id=1, source_target_pairs={{1,0},{2,1},{3,2},{5,4},{6,5},{7,6},{9,8},{10,9},{11,10},{13,12},{... | collective-permute-start | bytes 31208 | tf_op jit(solution)/shard_map/ppermute | solution.py:23
  89.0 6.1 %collective-permute-start.11 = (f32[2,10,130,1]{2,0,3,1:T(2,128)S(1)}, f32[2,10,130,1]{2,0,3,1:T(2,128)S(1)}, u32[]{:S(2)}, u32[]{:S(2)}) collective-permute-start(f32[2,10,130,1]{2,0,3,1:T(2,128)S(1)} %copy.263), channel_id=1, source_target_pairs={{0,1},{1,2},{2,3},{4,5},{5,6},{6,7},{8,9},{9,10},{10,11},{12,13},{... | collective-permute-start | bytes 31208 | tf_op jit(solution)/shard_map/ppermute | solution.py:22
  96.7 3.4 %copy-start.4 = (f32[8,128,128]{2,1,0:T(8,128)S(1)}, f32[8,128,128]{2,1,0:T(8,128)}, u32[]{:S(2)}) copy-start(f32[8,128,128]{2,1,0:T(8,128)} %param.7) | copy-start | bytes 1572868
  100.5 6.0 %copy-start.6 = (f32[24,48,50]{1,2,0:T(8,128)S(1)}, f32[24,48,50]{1,2,0:T(8,128)}, u32[]{:S(2)}) copy-start(f32[24,48,50]{1,2,0:T(8,128)} %copy.275) | copy-start | bytes 691204
  100.5 8.6 %collective-permute-start.12 = (f32[2,1,128,128]{3,2,1,0:T(8,128)S(1)}, f32[2,1,128,128]{3,2,1,0:T(8,128)S(1)}, u32[]{:S(2)}, u32[]{:S(2)}) collective-permute-start(f32[2,1,128,128]{3,2,1,0:T(8,128)S(1)} %get-tuple-element.43), channel_id=1, source_target_pairs={{16,0},{17,1},{18,2},{19,3},{20,4},{21,5},{22,6},{23,7},{24,8},{25... | collective-permute-start | bytes 393224 | tf_op jit(solution)/shard_map/ppermute | solution.py:23
  102.0 8.3 %collective-permute-start.13 = (f32[2,1,128,128]{3,2,1,0:T(8,128)S(1)}, f32[2,1,128,128]{3,2,1,0:T(8,128)S(1)}, u32[]{:S(2)}, u32[]{:S(2)}) collective-permute-start(f32[2,1,128,128]{3,2,1,0:T(8,128)S(1)} %get-tuple-element.42), channel_id=1, source_target_pairs={{0,16},{1,17},{2,18},{3,19},{4,20},{5,21},{6,22},{7,23},{8,24},{9,... | collective-permute-start | bytes 393224 | tf_op jit(solution)/shard_map/ppermute | solution.py:22
  110.3 7.2 %collective-permute-start.14 = (f32[2,10,1,128]{3,0,2,1:T(2,128)S(1)}, f32[2,10,1,128]{3,0,2,1:T(2,128)S(1)}, u32[]{:S(2)}, u32[]{:S(2)}) collective-permute-start(f32[2,10,1,128]{3,0,2,1:T(2,128)S(1)} %copy.265), channel_id=1, source_target_pairs={{4,0},{8,4},{12,8},{5,1},{9,5},{13,9},{6,2},{10,6},{14,10},{7,3},{... | collective-permute-start | bytes 30728 | tf_op jit(solution)/shard_map/ppermute | solution.py:23
  111.6 6.2 %collective-permute-start.15 = (f32[2,10,1,128]{3,0,2,1:T(2,128)S(1)}, f32[2,10,1,128]{3,0,2,1:T(2,128)S(1)}, u32[]{:S(2)}, u32[]{:S(2)}) collective-permute-start(f32[2,10,1,128]{3,0,2,1:T(2,128)S(1)} %copy.267), channel_id=1, source_target_pairs={{0,4},{4,8},{8,12},{1,5},{5,9},{9,13},{2,6},{6,10},{10,14},{3,7},{... | collective-permute-start | bytes 30728 | tf_op jit(solution)/shard_map/ppermute | solution.py:22
  117.5 54.2 %copy-start.1 = (f32[8,32,384]{2,1,0:T(8,128)}, f32[8,32,384]{2,1,0:T(8,128)S(1)}, u32[]{:S(2)}) copy-start(f32[8,32,384]{2,1,0:T(8,128)S(1)} %constant_dynamic-slice_fusion.2) | copy-start | bytes 1179652
  122.1 12.4 %collective-permute-start.16 = (f32[2,10,130,1]{2,0,3,1:T(2,128)S(1)}, f32[2,10,130,1]{2,0,3,1:T(2,128)S(1)}, u32[]{:S(2)}, u32[]{:S(2)}) collective-permute-start(f32[2,10,130,1]{2,0,3,1:T(2,128)S(1)} %copy.271), channel_id=1, source_target_pairs={{1,0},{2,1},{3,2},{5,4},{6,5},{7,6},{9,8},{10,9},{11,10},{13,12},{... | collective-permute-start | bytes 31208 | tf_op jit(solution)/shard_map/ppermute | solution.py:23
  125.5 10.6 %collective-permute-start.17 = (f32[2,10,130,1]{2,0,3,1:T(2,128)S(1)}, f32[2,10,130,1]{2,0,3,1:T(2,128)S(1)}, u32[]{:S(2)}, u32[]{:S(2)}) collective-permute-start(f32[2,10,130,1]{2,0,3,1:T(2,128)S(1)} %copy.273), channel_id=1, source_target_pairs={{0,1},{1,2},{2,3},{4,5},{5,6},{6,7},{8,9},{9,10},{10,11},{12,13},{... | collective-permute-start | bytes 31208 | tf_op jit(solution)/shard_map/ppermute | solution.py:22
  128.5 43.2 %copy-start.10 = (f32[1,32,384]{2,1,0:T(8,128)}, f32[1,32,384]{2,1,0:T(8,128)S(1)}, u32[]{:S(2)}) copy-start(f32[1,32,384]{2,1,0:T(8,128)S(1)} %collective-permute-done.18) | copy-start | bytes 147460
  129.9 41.8 %collective-permute-start.20 = (f32[10,1,384]{2,1,0:T(1,128)}, f32[10,1,384]{2,1,0:T(1,128)S(1)}, u32[]{:S(2)}, u32[]{:S(2)}) collective-permute-start(f32[10,1,384]{2,1,0:T(1,128)} %get-tuple-element.56), channel_id=1, source_target_pairs={{1,0},{2,1},{3,2},{4,3},{5,4},{6,5},{7,6},{8,7},{9,8},{10,9},{11,1... | collective-permute-start | bytes 46088 | tf_op jit(solution)/shard_map/ppermute | solution.py:23
  131.2 40.5 %collective-permute-start.21 = (f32[10,1,384]{2,1,0:T(1,128)}, f32[10,1,384]{2,1,0:T(1,128)S(1)}, u32[]{:S(2)}, u32[]{:S(2)}) collective-permute-start(f32[10,1,384]{2,1,0:T(1,128)} %get-tuple-element.57), channel_id=1, source_target_pairs={{0,1},{1,2},{2,3},{3,4},{4,5},{5,6},{6,7},{7,8},{8,9},{9,10},{10,1... | collective-permute-start | bytes 46088 | tf_op jit(solution)/shard_map/ppermute | solution.py:22
  143.7 30.1 %all-to-all-start = ((f32[8,128,128]{2,0,1:T(8,128)}), f32[8,128,128]{2,0,1:T(8,128)}, u32[]{:S(2)}, u32[]{:S(2)}) async-start(f32[8,128,128]{2,0,1:T(8,128)} %copy.283), calls=%async_computation | async-start | bytes 1048576 | tf_op jit(solution)/shard_map/all_to_all | solution.py:142
  147.9 106.5 %all-gather.2.cloned.1.call-start = ((), (), s32[]{:S(2)}) async-start(), calls=%async_computation.1 | async-start | bytes 1966080 | tf_op jit(solution)/shard_map/all_gather | solution.py:158
  171.7 4.3 %copy-start.14 = (f32[10,1,384]{2,1,0:T(1,128)}, f32[10,1,384]{2,1,0:T(1,128)S(1)}, u32[]{:S(2)}) copy-start(f32[10,1,384]{2,1,0:T(1,128)S(1)} %collective-permute-done.21) | copy-start | bytes 46084
  173.8 3.5 %copy-start.11 = (f32[1,32,384]{2,1,0:T(8,128)S(1)}, f32[1,32,384]{2,1,0:T(8,128)}, u32[]{:S(2)}) copy-start(f32[1,32,384]{2,1,0:T(8,128)} %copy-done.10) | copy-start | bytes 147460
  180.3 6.0 %collective-permute-start.22 = (f32[1,32,384]{2,1,0:T(8,128)S(1)}, f32[1,32,384]{2,1,0:T(8,128)S(1)}, u32[]{:S(2)}, u32[]{:S(2)}) collective-permute-start(f32[1,32,384]{2,1,0:T(8,128)S(1)} %get-tuple-element.63), channel_id=1, source_target_pairs={{16,0},{17,1},{18,2},{19,3},{20,4},{21,5},{22,6},{23,7},{24,8},{25... | collective-permute-start | bytes 147464 | tf_op jit(solution)/shard_map/ppermute | solution.py:23
  181.6 6.3 %collective-permute-start.23 = (f32[1,32,384]{2,1,0:T(8,128)S(1)}, f32[1,32,384]{2,1,0:T(8,128)S(1)}, u32[]{:S(2)}, u32[]{:S(2)}) collective-permute-start(f32[1,32,384]{2,1,0:T(8,128)S(1)} %get-tuple-element.62), channel_id=1, source_target_pairs={{0,16},{1,17},{2,18},{3,19},{4,20},{5,21},{6,22},{7,23},{8,24},{9,... | collective-permute-start | bytes 147464 | tf_op jit(solution)/shard_map/ppermute | solution.py:22
  187.9 4.6 %collective-permute-start.24 = (f32[10,1,384]{2,1,0:T(1,128)S(1)}, f32[10,1,384]{2,1,0:T(1,128)S(1)}, u32[]{:S(2)}, u32[]{:S(2)}) collective-permute-start(f32[10,1,384]{2,1,0:T(1,128)S(1)} %get-tuple-element.54), channel_id=1, source_target_pairs={{1,0},{2,1},{3,2},{4,3},{5,4},{6,5},{7,6},{8,7},{9,8},{10,9},{11,1... | collective-permute-start | bytes 46088 | tf_op jit(solution)/shard_map/ppermute | solution.py:23
  189.2 4.1 %collective-permute-start.25 = (f32[10,1,384]{2,1,0:T(1,128)S(1)}, f32[10,1,384]{2,1,0:T(1,128)S(1)}, u32[]{:S(2)}, u32[]{:S(2)}) collective-permute-start(f32[10,1,384]{2,1,0:T(1,128)S(1)} %get-tuple-element.55), channel_id=1, source_target_pairs={{0,1},{1,2},{2,3},{3,4},{4,5},{5,6},{6,7},{7,8},{8,9},{9,10},{10,1... | collective-permute-start | bytes 46088 | tf_op jit(solution)/shard_map/ppermute | solution.py:22
  194.6 6.0 %collective-permute-start.26 = (f32[1,32,384]{2,1,0:T(8,128)S(1)}, f32[1,32,384]{2,1,0:T(8,128)S(1)}, u32[]{:S(2)}, u32[]{:S(2)}) collective-permute-start(f32[1,32,384]{2,1,0:T(8,128)S(1)} %get-tuple-element.61), channel_id=1, source_target_pairs={{16,0},{17,1},{18,2},{19,3},{20,4},{21,5},{22,6},{23,7},{24,8},{25... | collective-permute-start | bytes 147464 | tf_op jit(solution)/shard_map/ppermute | solution.py:23
  195.9 6.3 %collective-permute-start.27 = (f32[1,32,384]{2,1,0:T(8,128)S(1)}, f32[1,32,384]{2,1,0:T(8,128)S(1)}, u32[]{:S(2)}, u32[]{:S(2)}) collective-permute-start(f32[1,32,384]{2,1,0:T(8,128)S(1)} %get-tuple-element.60), channel_id=1, source_target_pairs={{0,16},{1,17},{2,18},{3,19},{4,20},{5,21},{6,22},{7,23},{8,24},{9,... | collective-permute-start | bytes 147464 | tf_op jit(solution)/shard_map/ppermute | solution.py:22
  202.2 4.5 %collective-permute-start.28 = (f32[10,1,384]{2,1,0:T(1,128)S(1)}, f32[10,1,384]{2,1,0:T(1,128)S(1)}, u32[]{:S(2)}, u32[]{:S(2)}) collective-permute-start(f32[10,1,384]{2,1,0:T(1,128)S(1)} %get-tuple-element.52), channel_id=1, source_target_pairs={{1,0},{2,1},{3,2},{4,3},{5,4},{6,5},{7,6},{8,7},{9,8},{10,9},{11,1... | collective-permute-start | bytes 46088 | tf_op jit(solution)/shard_map/ppermute | solution.py:23
  203.5 4.0 %collective-permute-start.29 = (f32[10,1,384]{2,1,0:T(1,128)S(1)}, f32[10,1,384]{2,1,0:T(1,128)S(1)}, u32[]{:S(2)}, u32[]{:S(2)}) collective-permute-start(f32[10,1,384]{2,1,0:T(1,128)S(1)} %get-tuple-element.53), channel_id=1, source_target_pairs={{0,1},{1,2},{2,3},{3,4},{4,5},{5,6},{6,7},{7,8},{8,9},{9,10},{10,1... | collective-permute-start | bytes 46088 | tf_op jit(solution)/shard_map/ppermute | solution.py:22
  208.8 6.0 %collective-permute-start.30 = (f32[1,32,384]{2,1,0:T(8,128)S(1)}, f32[1,32,384]{2,1,0:T(8,128)S(1)}, u32[]{:S(2)}, u32[]{:S(2)}) collective-permute-start(f32[1,32,384]{2,1,0:T(8,128)S(1)} %get-tuple-element.59), channel_id=1, source_target_pairs={{16,0},{17,1},{18,2},{19,3},{20,4},{21,5},{22,6},{23,7},{24,8},{25... | collective-permute-start | bytes 147464 | tf_op jit(solution)/shard_map/ppermute | solution.py:23
  210.1 6.3 %collective-permute-start.31 = (f32[1,32,384]{2,1,0:T(8,128)S(1)}, f32[1,32,384]{2,1,0:T(8,128)S(1)}, u32[]{:S(2)}, u32[]{:S(2)}) collective-permute-start(f32[1,32,384]{2,1,0:T(8,128)S(1)} %get-tuple-element.58), channel_id=1, source_target_pairs={{0,16},{1,17},{2,18},{3,19},{4,20},{5,21},{6,22},{7,23},{8,24},{9,... | collective-permute-start | bytes 147464 | tf_op jit(solution)/shard_map/ppermute | solution.py:22
  216.4 6.2 %collective-permute-start.32 = (f32[10,1,384]{2,1,0:T(1,128)S(1)}, f32[10,1,384]{2,1,0:T(1,128)S(1)}, u32[]{:S(2)}, u32[]{:S(2)}) collective-permute-start(f32[10,1,384]{2,1,0:T(1,128)S(1)} %get-tuple-element.50), channel_id=1, source_target_pairs={{1,0},{2,1},{3,2},{4,3},{5,4},{6,5},{7,6},{8,7},{9,8},{10,9},{11,1... | collective-permute-start | bytes 46088 | tf_op jit(solution)/shard_map/ppermute | solution.py:23
  217.7 5.7 %collective-permute-start.33 = (f32[10,1,384]{2,1,0:T(1,128)S(1)}, f32[10,1,384]{2,1,0:T(1,128)S(1)}, u32[]{:S(2)}, u32[]{:S(2)}) collective-permute-start(f32[10,1,384]{2,1,0:T(1,128)S(1)} %get-tuple-element.51), channel_id=1, source_target_pairs={{0,1},{1,2},{2,3},{3,4},{4,5},{5,6},{6,7},{7,8},{8,9},{9,10},{10,1... | collective-permute-start | bytes 46088 | tf_op jit(solution)/shard_map/ppermute | solution.py:22
  (4 other events, 6.8 us)
Sparse Core Ops, SparseCore 0:
  225.8 28.5 all-gather.1
where the time goes:
time: 266 us; the launch traced here: 264 us
  starting transfers between devices  98.2 us (37%)
  local copies, waits for them, and re-layouts  78.9 us (30%)
  waiting for transfers between devices  41 us (15%)
  other arithmetic  30.4 us (11%)
  between operations  15.5 us (6%)
    ppermute x17, starting transfers between devices, padded(): before = lax.ppermute(last, axis, up)  71.7 us
    all_gather x1, waiting for transfers between devices, on_device(): segment_kelvin = lax.all_gather(segment_kelvin, 'gx', axis=1, tiled=True)  27.3 us
    ppermute x17, starting transfers between devices, padded(): after = lax.ppermute(first, axis, down)  22.1 us
    unnamed x43, local copies, waits for them, and re-layouts  17.8 us
    slice x9, local copies, waits for them, and re-layouts, padded(): first = lax.slice_in_dim(value, 0, width, axis=dim)  14.4 us
    add x3, other arithmetic, neighbours(): total + bordered_segment[:, 1:-1, 1:-1, 2:]  14 us
    slice x1, local copies, waits for them, and re-layouts, diffusivity_coefficient(): centre_mask = bordered_segment_flags[1:-1, 1:-1, 1:-1]  12 us
    ppermute x17, waiting for transfers between devices, padded(): before = lax.ppermute(last, axis, up)  9.99 us
  transfers between devices with their start and end apart: 36, of which 14 were waited for; matrix products, arithmetic and copies ran while one was open for 27% of the time, Pallas kernels for 0%

commit v1 on v0

--- a/solution.py
+++ b/solution.py
@@ -10,6 +10,12 @@
 HEATING = 0.02
 CONDUCT = 0.16
 SOFTEN = 0.25
+
+
+def laid_out(blocks, dim):
+    shape = list(blocks.shape[1:])
+    shape[dim] *= blocks.shape[0]
+    return jnp.moveaxis(blocks, 0, dim).reshape(shape)
 
 
 def padded(value, sides, width):
@@ -155,7 +161,19 @@
             bordered_segment_flags,
             block_heat_source,
         )
-    segment_kelvin = lax.all_gather(segment_kelvin, "gx", axis=1, tiled=True)
+    size = lax.axis_size("gx")
+    pairs = [(i_2, (i_2 + 1) % size) for i_2 in range(size)]
+    back = [(b, a) for a, b in pairs]
+    lower, upper = ([], [])
+    for step in range(size - 1):
+        if step % 2 == 0:
+            lower.append(lax.ppermute(lower[-1] if lower else segment_kelvin, "gx", pairs))
+        else:
+            upper.append(lax.ppermute(upper[-1] if upper else segment_kelvin, "gx", back))
+    pieces = jnp.stack([*lower[::-1], segment_kelvin, *upper])
+    shift = lax.axis_index("gx") - len(lower)
+    pieces = pieces[(jnp.arange(size) - shift) % size]
+    segment_kelvin = laid_out(pieces, 1)
     return (magnetic_curl_state, segment_kelvin)
 
 

time: 266 us -> 251 us (0.944)
  the two profiles are of different devices: /device:TPU:0 before, /device:TPU:26 now
where the time goes in v1:
time: 251 us; the launch traced here: 249 us
  starting transfers between devices  80.7 us (32%)
  local copies, waits for them, and re-layouts  74.9 us (30%)
  waiting for transfers between devices  55.4 us (22%)
  other arithmetic  35.5 us (14%)
    ppermute x17, starting transfers between devices, padded(): after = lax.ppermute(first, axis, down)  42.7 us
    ppermute x17, waiting for transfers between devices, padded(): before = lax.ppermute(last, axis, up)  39.4 us
    ppermute x17, starting transfers between devices, padded(): before = lax.ppermute(last, axis, up)  31.9 us
    unnamed x36, local copies, waits for them, and re-layouts  15.6 us
    ppermute x2, waiting for transfers between devices, on_device(): lax.ppermute(lower[-1] if lower else segment_kelvin, 'gx', pairs)  14.6 us
    slice x9, local copies, waits for them, and re-layouts, padded(): first = lax.slice_in_dim(value, 0, width, axis=dim)  14.4 us
    add x3, other arithmetic, neighbours(): total + bordered_segment[:, 1:-1, 1:-1, 2:]  14.4 us
    slice x1, local copies, waits for them, and re-layouts, diffusivity_coefficient(): centre_mask = bordered_segment_flags[1:-1, 1:-1, 1:-1]  12.1 us
  transfers between devices with their start and end apart: 38, of which 15 were waited for; matrix products, arithmetic and copies ran while one was open for 30% of the time, Pallas kernels for 0%

profile of v1, /device:TPU:26, one launch (start us, length us, event | category | flops | bytes accessed | tf_op | source)
XLA Modules:
  0.0 248.6 jit_solution(9370197840706611393)
XLA Ops:
  0.6 2.0 copy.327
  4.7 4.6 %collective-permute-start = (f32[2,1,128,128]{3,0,2,1:T(2,128)}, f32[2,1,128,128]{3,0,2,1:T(2,128)S(1)}, u32[]{:S(2)}, u32[]{:S(2)}) collective-permute-start(f32[2,1,128,128]{3,0,2,1:T(2,128)} %get-tuple-element.40), channel_id=1, source_target_pairs={{16,0},{17,1},{18,2},{19,3},{20,4},{21,5},{22,6},{23,7},{24,8},{25... | collective-permute-start | bytes 393224 | tf_op jit(solution)/shard_map/ppermute | solution.py:29
  13.9 2.4 collective-permute-start.2
  18.2 3.6 %collective-permute-done.3 = f32[2,10,1,128]{3,0,2,1:T(2,128)S(1)} collective-permute-done((f32[2,10,1,128]{3,0,2,1:T(2,128)S(1)}, f32[2,10,1,128]{3,0,2,1:T(2,128)S(1)}, u32[]{:S(2)}, u32[]{:S(2)}) %collective-permute-start.3) | collective-permute-done | bytes 10272 | tf_op jit(solution)/shard_map/ppermute | solution.py:28
  23.7 3.0 %fusion.215 = (f32[2,10,130,1]{3,0,2,1:T(2,128)}, f32[2,10,130,1]{3,0,2,1:T(2,128)}) fusion(f32[2,10,130,128]{3,0,2,1:T(2,128)S(1)} %pad_maximum_fusion.3), kind=kLoop, calls=%fused_computation.419 | loop fusion | bytes 41600 | tf_op jit(solution)/shard_map/slice | solution.py:27
  26.7 2.5 %copy.331 = f32[2,10,130,1]{2,0,3,1:T(2,128)} copy(f32[2,10,130,1]{3,0,2,1:T(2,128)} %get-tuple-element.26) | data formatting | bytes 20800 | tf_op jit(solution)/shard_map/slice | solution.py:27
  30.5 2.5 %copy.333 = f32[2,10,130,1]{2,0,3,1:T(2,128)} copy(f32[2,10,130,1]{3,0,2,1:T(2,128)} %get-tuple-element.27) | data formatting | bytes 20800 | tf_op jit(solution)/shard_map/slice | solution.py:26
  33.0 3.6 %collective-permute-start.5 = (f32[2,10,130,1]{2,0,3,1:T(2,128)}, f32[2,10,130,1]{2,0,3,1:T(2,128)}, u32[]{:S(2)}, u32[]{:S(2)}) collective-permute-start(f32[2,10,130,1]{2,0,3,1:T(2,128)} %copy.333), channel_id=1, source_target_pairs={{0,1},{1,2},{2,3},{4,5},{5,6},{6,7},{8,9},{9,10},{10,11},{12,13},{... | collective-permute-start | bytes 31208 | tf_op jit(solution)/shard_map/ppermute | solution.py:28
  36.8 2.4 copy.332
  39.2 2.4 copy.334
  41.7 7.6 %fusion.10 = f32[2,8,128,128]{3,0,2,1:T(2,128)S(1)} fusion(f32[2,10,130,1]{3,0,2,1:T(2,128)} %copy.334, f32[2,10,1,128]{3,0,2,1:T(2,128)S(1)} %collective-permute-done.2, f32[2,10,128,128]{3,0,2,1:T(2,128)} %copy-done.2, f32[2,10,1,128]{3,0,2,1:T(2,128)S(1)} %copy-done.11, f32[2,10,130,1]{3,0,2,1:T(2,128)} %copy.332, f32[2,8,128,128]{3,0,2,1:T(2,128)S(1)} %copy.327, ...), kind=kLoop, calls=%fused_computation.67 | loop fusion | flops 3932160 | bytes 3711296 | tf_op jit(solution)/shard_map/add | solution.py:43
  50.8 3.6 %collective-permute-start.6 = (f32[2,1,128,128]{3,2,1,0:T(8,128)S(1)}, f32[2,1,128,128]{3,2,1,0:T(8,128)S(1)}, u32[]{:S(2)}, u32[]{:S(2)}) collective-permute-start(f32[2,1,128,128]{3,2,1,0:T(8,128)S(1)} %get-tuple-element.37), channel_id=1, source_target_pairs={{16,0},{17,1},{18,2},{19,3},{20,4},{21,5},{22,6},{23,7},{24,8},{25... | collective-permute-start | bytes 393224 | tf_op jit(solution)/shard_map/ppermute | solution.py:29
  57.2 5.2 %collective-permute-start.18 = (f32[1,32,384]{2,1,0:T(8,128)}, f32[1,32,384]{2,1,0:T(8,128)}, u32[]{:S(2)}, u32[]{:S(2)}) collective-permute-start(f32[1,32,384]{2,1,0:T(8,128)} %get-tuple-element.21), channel_id=1, source_target_pairs={{16,0},{17,1},{18,2},{19,3},{20,4},{21,5},{22,6},{23,7},{24,8},{25... | collective-permute-start | bytes 147464 | tf_op jit(solution)/shard_map/ppermute | solution.py:29
  63.8 2.4 collective-permute-start.8
  67.6 4.2 %collective-permute-done.9 = f32[2,10,1,128]{3,0,2,1:T(2,128)S(1)} collective-permute-done((f32[2,10,1,128]{3,0,2,1:T(2,128)S(1)}, f32[2,10,1,128]{3,0,2,1:T(2,128)S(1)}, u32[]{:S(2)}, u32[]{:S(2)}) %collective-permute-start.9) | collective-permute-done | bytes 10272 | tf_op jit(solution)/shard_map/ppermute | solution.py:28
  71.9 2.0 fusion.214
  73.9 2.1 copy.342
  77.3 2.1 copy.344
  79.4 3.2 %collective-permute-start.11 = (f32[2,10,130,1]{2,0,3,1:T(2,128)S(1)}, f32[2,10,130,1]{2,0,3,1:T(2,128)S(1)}, u32[]{:S(2)}, u32[]{:S(2)}) collective-permute-start(f32[2,10,130,1]{2,0,3,1:T(2,128)S(1)} %copy.344), channel_id=1, source_target_pairs={{0,1},{1,2},{2,3},{4,5},{5,6},{6,7},{8,9},{9,10},{10,11},{12,13},{... | collective-permute-start | bytes 31208 | tf_op jit(solution)/shard_map/ppermute | solution.py:28
  87.1 3.4 %fusion.5 = f32[2,8,128,128]{3,2,1,0:T(8,128)S(1)} fusion(f32[2,10,130,1]{3,2,1,0:T(8,128)} %copy.345, f32[2,10,1,128]{3,2,1,0:T(1,128)S(1)} %copy.337, f32[2,10,1,128]{3,2,1,0:T(1,128)S(1)} %copy.339, f32[2,1,128,128]{3,2,1,0:T(8,128)S(1)} %collective-permute-done.6, f32[2,1,128,128]{3,2,1,0:T(8,128)S(1)} %collective-permute-done.7, ...), kind=kLoop, calls=%fused_computation.38 | loop fusion | flops 7602176 | bytes 2400576 | tf_op jit(solution)/shard_map/add | solution.py:43
  91.0 5.3 %collective-permute-start.12 = (f32[2,1,128,128]{3,2,1,0:T(8,128)S(1)}, f32[2,1,128,128]{3,2,1,0:T(8,128)S(1)}, u32[]{:S(2)}, u32[]{:S(2)}) collective-permute-start(f32[2,1,128,128]{3,2,1,0:T(8,128)S(1)} %get-tuple-element.35), channel_id=1, source_target_pairs={{16,0},{17,1},{18,2},{19,3},{20,4},{21,5},{22,6},{23,7},{24,8},{25... | collective-permute-start | bytes 393224 | tf_op jit(solution)/shard_map/ppermute | solution.py:29
  97.6 2.6 %broadcast_bitcast_fusion = f32[24,48,400]{1,2,0:T(8,128)} fusion(f32[24,48,50]{1,2,0:T(8,128)S(1)} %copy-done.6), kind=kLoop, calls=%fused_computation.1 | loop fusion | bytes 2073600 | tf_op jit(solution)/shard_map/convert_element_type | solution.py:37
  100.1 4.3 %collective-permute-done.13 = f32[2,1,128,128]{3,2,1,0:T(8,128)S(1)} collective-permute-done((f32[2,1,128,128]{3,2,1,0:T(8,128)S(1)}, f32[2,1,128,128]{3,2,1,0:T(8,128)S(1)}, u32[]{:S(2)}, u32[]{:S(2)}) %collective-permute-start.13) | collective-permute-done | bytes 131104 | tf_op jit(solution)/shard_map/ppermute | solution.py:28
  104.4 2.4 collective-permute-start.14
  109.2 3.2 %collective-permute-done.15 = f32[2,10,1,128]{3,0,2,1:T(2,128)S(1)} collective-permute-done((f32[2,10,1,128]{3,0,2,1:T(2,128)S(1)}, f32[2,10,1,128]{3,0,2,1:T(2,128)S(1)}, u32[]{:S(2)}, u32[]{:S(2)}) %collective-permute-start.15) | collective-permute-done | bytes 10272 | tf_op jit(solution)/shard_map/ppermute | solution.py:28
  112.5 2.0 fusion.213
  114.5 2.1 copy.352
  117.9 2.1 copy.354
  120.0 3.0 %collective-permute-start.17 = (f32[2,10,130,1]{2,0,3,1:T(2,128)S(1)}, f32[2,10,130,1]{2,0,3,1:T(2,128)S(1)}, u32[]{:S(2)}, u32[]{:S(2)}) collective-permute-start(f32[2,10,130,1]{2,0,3,1:T(2,128)S(1)} %copy.354), channel_id=1, source_target_pairs={{0,1},{1,2},{2,3},{4,5},{5,6},{6,7},{8,9},{9,10},{10,11},{12,13},{... | collective-permute-start | bytes 31208 | tf_op jit(solution)/shard_map/ppermute | solution.py:28
  126.4 2.4 collective-permute-start.21
  132.0 3.4 %fusion = f32[2,8,128,128]{3,2,1,0:T(8,128)S(1)} fusion(f32[2,10,130,1]{3,2,1,0:T(8,128)} %copy.355, f32[2,10,1,128]{3,2,1,0:T(1,128)S(1)} %copy.347, f32[2,10,1,128]{3,2,1,0:T(1,128)S(1)} %copy.349, f32[2,1,128,128]{3,2,1,0:T(8,128)S(1)} %collective-permute-done.12, f32[2,1,128,128]{3,2,1,0:T(8,128)S(1)} %collective-permute-done.13, ...), kind=kLoop, calls=%fused_computation.9 | loop fusion | flops 7602176 | bytes 2400576 | tf_op jit(solution)/shard_map/add | solution.py:43
  138.1 4.4 %all-to-all-start = ((f32[8,128,128]{2,0,1:T(8,128)}), f32[8,128,128]{2,0,1:T(8,128)}, u32[]{:S(2)}, u32[]{:S(2)}) async-start(f32[8,128,128]{2,0,1:T(8,128)} %copy.364), calls=%async_computation | async-start | bytes 1048576 | tf_op jit(solution)/shard_map/all_to_all | solution.py:148
  142.4 12.1 %fusion.212 = (f32[8,32,384]{1,2,0:T(8,128)}, f32[8,32,384]{1,2,0:T(8,128)}, f32[8,32,384]{1,2,0:T(8,128)}, f32[8,32,384]{1,2,0:T(8,128)S(1)}, f32[8,32,384]{1,2...) fusion(f32[24,48,400]{1,2,0:T(8,128)} %broadcast_bitcast_fusion), kind=kLoop, calls=%fused_computation.416 | loop fusion | bytes 5505024 | tf_op jit(solution)/shard_map/slice | solution.py:76
  166.2 2.1 select_maximum_fusion.12
  168.3 2.2 copy.377
  171.7 3.0 %fusion.47 = f32[8,32,384]{2,1,0:T(8,128)S(1)} fusion(f32[8,32,384]{2,1,0:T(8,128)} %copy-done.1, f32[8,32,384]{2,1,0:T(8,128)S(1)} %copy.369, f32[8,32,384]{2,1,0:T(8,128)S(1)} %copy.370, f32[8,32,384]{2,1,0:T(8,128)S(1)} %copy.371, f32[8,32,384]{2,1,0:T(8,128)S(1)} %copy.372, f32[8,32,384]{2,1,0:T(8,128)S(1)} %copy.373, f32[8,32,384]{2,1,0:T(8,128)S(1)} %copy.374, ...), kind=kLoop, calls=%fused_computation.178 | loop fusion | flops 6782976 | bytes 4847616 | tf_op jit(solution)/shard_map/add | solution.py:82
  178.0 4.6 %collective-permute-done.23 = f32[1,32,384]{2,1,0:T(8,128)S(1)} collective-permute-done((f32[1,32,384]{2,1,0:T(8,128)S(1)}, f32[1,32,384]{2,1,0:T(8,128)S(1)}, u32[]{:S(2)}, u32[]{:S(2)}) %collective-permute-start.23) | collective-permute-done | bytes 49184 | tf_op jit(solution)/shard_map/ppermute | solution.py:28
  182.6 2.7 %collective-permute-start.24 = (f32[10,1,384]{2,1,0:T(1,128)S(1)}, f32[10,1,384]{2,1,0:T(1,128)S(1)}, u32[]{:S(2)}, u32[]{:S(2)}) collective-permute-start(f32[10,1,384]{2,1,0:T(1,128)S(1)} %get-tuple-element.46), channel_id=1, source_target_pairs={{1,0},{2,1},{3,2},{4,3},{5,4},{6,5},{7,6},{8,7},{9,8},{10,9},{11,1... | collective-permute-start | bytes 46088 | tf_op jit(solution)/shard_map/ppermute | solution.py:29
  187.3 4.0 %collective-permute-done.25 = f32[10,1,384]{2,1,0:T(1,128)S(1)} collective-permute-done((f32[10,1,384]{2,1,0:T(1,128)S(1)}, f32[10,1,384]{2,1,0:T(1,128)S(1)}, u32[]{:S(2)}, u32[]{:S(2)}) %collective-permute-start.25) | collective-permute-done | bytes 15392 | tf_op jit(solution)/shard_map/ppermute | solution.py:28
  196.0 4.3 %collective-permute-done.27 = f32[1,32,384]{2,1,0:T(8,128)S(1)} collective-permute-done((f32[1,32,384]{2,1,0:T(8,128)S(1)}, f32[1,32,384]{2,1,0:T(8,128)S(1)}, u32[]{:S(2)}, u32[]{:S(2)}) %collective-permute-start.27) | collective-permute-done | bytes 49184 | tf_op jit(solution)/shard_map/ppermute | solution.py:28
  202.2 2.4 collective-permute-start.29
  204.6 3.5 %collective-permute-done.29 = f32[10,1,384]{2,1,0:T(1,128)S(1)} collective-permute-done((f32[10,1,384]{2,1,0:T(1,128)S(1)}, f32[10,1,384]{2,1,0:T(1,128)S(1)}, u32[]{:S(2)}, u32[]{:S(2)}) %collective-permute-start.29) | collective-permute-done | bytes 15392 | tf_op jit(solution)/shard_map/ppermute | solution.py:28
  212.8 4.3 %collective-permute-done.31 = f32[1,32,384]{2,1,0:T(8,128)S(1)} collective-permute-done((f32[1,32,384]{2,1,0:T(8,128)S(1)}, f32[1,32,384]{2,1,0:T(8,128)S(1)}, u32[]{:S(2)}, u32[]{:S(2)}) %collective-permute-start.31) | collective-permute-done | bytes 49184 | tf_op jit(solution)/shard_map/ppermute | solution.py:28
  219.0 2.4 collective-permute-start.33
  221.4 3.5 %collective-permute-done.33 = f32[10,1,384]{2,1,0:T(1,128)S(1)} collective-permute-done((f32[10,1,384]{2,1,0:T(1,128)S(1)}, f32[10,1,384]{2,1,0:T(1,128)S(1)}, u32[]{:S(2)}, u32[]{:S(2)}) %collective-permute-start.33) | collective-permute-done | bytes 15392 | tf_op jit(solution)/shard_map/ppermute | solution.py:28
  228.7 9.7 %collective-permute-done.34 = f32[8,32,384]{2,1,0:T(8,128)S(1)} collective-permute-done((f32[8,32,384]{2,1,0:T(8,128)}, f32[8,32,384]{2,1,0:T(8,128)S(1)}, u32[]{:S(2)}, u32[]{:S(2)}) %collective-permute-start.34) | collective-permute-done | bytes 393248 | tf_op jit(solution)/shard_map/ppermute | solution.py:170
  238.4 2.3 pad_maximum_fusion.62
  240.7 4.9 %collective-permute-done.35 = f32[8,32,384]{2,1,0:T(8,128)S(1)} collective-permute-done((f32[8,32,384]{2,1,0:T(8,128)S(1)}, f32[8,32,384]{2,1,0:T(8,128)S(1)}, u32[]{:S(2)}, u32[]{:S(2)}) %collective-permute-start.35) | collective-permute-done | bytes 393248 | tf_op jit(solution)/shard_map/ppermute | solution.py:170
  (144 shorter events, 76.7 us)
Async XLA Ops:
  2.7 9.2 %copy-start = (f32[2,8,128,128]{3,2,1,0:T(8,128)S(1)}, f32[2,8,128,128]{3,2,1,0:T(8,128)}, u32[]{:S(2)}) copy-start(f32[2,8,128,128]{3,2,1,0:T(8,128)} %param.6) | copy-start | bytes 3145732
  3.4 8.4 %collective-permute-start.1 = (f32[2,1,128,128]{3,0,2,1:T(2,128)}, f32[2,1,128,128]{3,0,2,1:T(2,128)S(1)}, u32[]{:S(2)}, u32[]{:S(2)}) collective-permute-start(f32[2,1,128,128]{3,0,2,1:T(2,128)} %get-tuple-element.41), channel_id=1, source_target_pairs={{0,16},{1,17},{2,18},{3,19},{4,20},{5,21},{6,22},{7,23},{8,24},{9,... | collective-permute-start | bytes 393224 | tf_op jit(solution)/shard_map/ppermute | solution.py:28
  4.7 8.1 %collective-permute-start = (f32[2,1,128,128]{3,0,2,1:T(2,128)}, f32[2,1,128,128]{3,0,2,1:T(2,128)S(1)}, u32[]{:S(2)}, u32[]{:S(2)}) collective-permute-start(f32[2,1,128,128]{3,0,2,1:T(2,128)} %get-tuple-element.40), channel_id=1, source_target_pairs={{16,0},{17,1},{18,2},{19,3},{20,4},{21,5},{22,6},{23,7},{24,8},{25... | collective-permute-start | bytes 393224 | tf_op jit(solution)/shard_map/ppermute | solution.py:29
  13.9 4.4 %collective-permute-start.2 = (f32[2,10,1,128]{3,0,2,1:T(2,128)S(1)}, f32[2,10,1,128]{3,0,2,1:T(2,128)S(1)}, u32[]{:S(2)}, u32[]{:S(2)}) collective-permute-start(f32[2,10,1,128]{3,0,2,1:T(2,128)S(1)} %get-tuple-element.33), channel_id=1, source_target_pairs={{4,0},{8,4},{12,8},{5,1},{9,5},{13,9},{6,2},{10,6},{14,10},{7,3},{... | collective-permute-start | bytes 30728 | tf_op jit(solution)/shard_map/ppermute | solution.py:29
  16.2 5.6 %collective-permute-start.3 = (f32[2,10,1,128]{3,0,2,1:T(2,128)S(1)}, f32[2,10,1,128]{3,0,2,1:T(2,128)S(1)}, u32[]{:S(2)}, u32[]{:S(2)}) collective-permute-start(f32[2,10,1,128]{3,0,2,1:T(2,128)S(1)} %get-tuple-element.32), channel_id=1, source_target_pairs={{0,4},{4,8},{8,12},{1,5},{5,9},{9,13},{2,6},{6,10},{10,14},{3,7},{... | collective-permute-start | bytes 30728 | tf_op jit(solution)/shard_map/ppermute | solution.py:28
  21.8 4.9 %copy-start.10 = (f32[2,10,1,128]{3,0,2,1:T(2,128)}, f32[2,10,1,128]{3,0,2,1:T(2,128)S(1)}, u32[]{:S(2)}) copy-start(f32[2,10,1,128]{3,0,2,1:T(2,128)S(1)} %collective-permute-done.3) | copy-start | bytes 30724
  26.7 10.0 %copy-start.12 = (f32[128,16]{0,1:T(8,128)S(1)}, f32[128,16]{0,1:T(8,128)}, u32[]{:S(2)}) copy-start(f32[128,16]{0,1:T(8,128)} %copy.324) | copy-start | bytes 24580
  29.2 7.6 %collective-permute-start.4 = (f32[2,10,130,1]{2,0,3,1:T(2,128)}, f32[2,10,130,1]{2,0,3,1:T(2,128)}, u32[]{:S(2)}, u32[]{:S(2)}) collective-permute-start(f32[2,10,130,1]{2,0,3,1:T(2,128)} %copy.331), channel_id=1, source_target_pairs={{1,0},{2,1},{3,2},{5,4},{6,5},{7,6},{9,8},{10,9},{11,10},{13,12},{... | collective-permute-start | bytes 31208 | tf_op jit(solution)/shard_map/ppermute | solution.py:29
  33.0 6.2 %collective-permute-start.5 = (f32[2,10,130,1]{2,0,3,1:T(2,128)}, f32[2,10,130,1]{2,0,3,1:T(2,128)}, u32[]{:S(2)}, u32[]{:S(2)}) collective-permute-start(f32[2,10,130,1]{2,0,3,1:T(2,128)} %copy.333), channel_id=1, source_target_pairs={{0,1},{1,2},{2,3},{4,5},{5,6},{6,7},{8,9},{9,10},{10,11},{12,13},{... | collective-permute-start | bytes 31208 | tf_op jit(solution)/shard_map/ppermute | solution.py:28
  36.8 53.7 %copy-start.7 = (f32[128,128]{1,0:T(8,128)}, f32[128,128]{1,0:T(8,128)S(1)}, u32[]{:S(2)}) copy-start(f32[128,128]{1,0:T(8,128)S(1)} %copy.325) | copy-start | bytes 196612
  36.8 4.9 %copy-start.11 = (f32[2,10,1,128]{3,0,2,1:T(2,128)S(1)}, f32[2,10,1,128]{3,0,2,1:T(2,128)}, u32[]{:S(2)}) copy-start(f32[2,10,1,128]{3,0,2,1:T(2,128)} %copy-done.10) | copy-start | bytes 30724
  50.8 12.8 %copy-start.9 = (s32[2,64,64]{2,1,0:T(8,128)S(1)}, s32[2,64,64]{2,1,0:T(8,128)}, u32[]{:S(2)}) copy-start(s32[2,64,64]{2,1,0:T(8,128)} %param.10) | copy-start | bytes 98308
  50.8 12.9 %collective-permute-start.6 = (f32[2,1,128,128]{3,2,1,0:T(8,128)S(1)}, f32[2,1,128,128]{3,2,1,0:T(8,128)S(1)}, u32[]{:S(2)}, u32[]{:S(2)}) collective-permute-start(f32[2,1,128,128]{3,2,1,0:T(8,128)S(1)} %get-tuple-element.37), channel_id=1, source_target_pairs={{16,0},{17,1},{18,2},{19,3},{20,4},{21,5},{22,6},{23,7},{24,8},{25... | collective-permute-start | bytes 393224 | tf_op jit(solution)/shard_map/ppermute | solution.py:29
  54.4 9.3 %collective-permute-start.7 = (f32[2,1,128,128]{3,2,1,0:T(8,128)S(1)}, f32[2,1,128,128]{3,2,1,0:T(8,128)S(1)}, u32[]{:S(2)}, u32[]{:S(2)}) collective-permute-start(f32[2,1,128,128]{3,2,1,0:T(8,128)S(1)} %get-tuple-element.36), channel_id=1, source_target_pairs={{0,16},{1,17},{2,18},{3,19},{4,20},{5,21},{6,22},{7,23},{8,24},{9,... | collective-permute-start | bytes 393224 | tf_op jit(solution)/shard_map/ppermute | solution.py:28
  57.2 65.9 %collective-permute-start.18 = (f32[1,32,384]{2,1,0:T(8,128)}, f32[1,32,384]{2,1,0:T(8,128)}, u32[]{:S(2)}, u32[]{:S(2)}) collective-permute-start(f32[1,32,384]{2,1,0:T(8,128)} %get-tuple-element.21), channel_id=1, source_target_pairs={{16,0},{17,1},{18,2},{19,3},{20,4},{21,5},{22,6},{23,7},{24,8},{25... | collective-permute-start | bytes 147464 | tf_op jit(solution)/shard_map/ppermute | solution.py:29
  62.3 60.7 %collective-permute-start.19 = (f32[1,32,384]{2,1,0:T(8,128)}, f32[1,32,384]{2,1,0:T(8,128)}, u32[]{:S(2)}, u32[]{:S(2)}) collective-permute-start(f32[1,32,384]{2,1,0:T(8,128)} %get-tuple-element.20), channel_id=1, source_target_pairs={{0,16},{1,17},{2,18},{3,19},{4,20},{5,21},{6,22},{7,23},{8,24},{9,... | collective-permute-start | bytes 147464 | tf_op jit(solution)/shard_map/ppermute | solution.py:28
  63.8 3.8 %collective-permute-start.8 = (f32[2,10,1,128]{3,0,2,1:T(2,128)S(1)}, f32[2,10,1,128]{3,0,2,1:T(2,128)S(1)}, u32[]{:S(2)}, u32[]{:S(2)}) collective-permute-start(f32[2,10,1,128]{3,0,2,1:T(2,128)S(1)} %copy.336), channel_id=1, source_target_pairs={{4,0},{8,4},{12,8},{5,1},{9,5},{13,9},{6,2},{10,6},{14,10},{7,3},{... | collective-permute-start | bytes 30728 | tf_op jit(solution)/shard_map/ppermute | solution.py:29
  66.2 5.6 %collective-permute-start.9 = (f32[2,10,1,128]{3,0,2,1:T(2,128)S(1)}, f32[2,10,1,128]{3,0,2,1:T(2,128)S(1)}, u32[]{:S(2)}, u32[]{:S(2)}) collective-permute-start(f32[2,10,1,128]{3,0,2,1:T(2,128)S(1)} %copy.338), channel_id=1, source_target_pairs={{0,4},{4,8},{8,12},{1,5},{5,9},{9,13},{2,6},{6,10},{10,14},{3,7},{... | collective-permute-start | bytes 30728 | tf_op jit(solution)/shard_map/ppermute | solution.py:28
  76.0 7.8 %collective-permute-start.10 = (f32[2,10,130,1]{2,0,3,1:T(2,128)S(1)}, f32[2,10,130,1]{2,0,3,1:T(2,128)S(1)}, u32[]{:S(2)}, u32[]{:S(2)}) collective-permute-start(f32[2,10,130,1]{2,0,3,1:T(2,128)S(1)} %copy.342), channel_id=1, source_target_pairs={{1,0},{2,1},{3,2},{5,4},{6,5},{7,6},{9,8},{10,9},{11,10},{13,12},{... | collective-permute-start | bytes 31208 | tf_op jit(solution)/shard_map/ppermute | solution.py:29
  79.4 6.1 %collective-permute-start.11 = (f32[2,10,130,1]{2,0,3,1:T(2,128)S(1)}, f32[2,10,130,1]{2,0,3,1:T(2,128)S(1)}, u32[]{:S(2)}, u32[]{:S(2)}) collective-permute-start(f32[2,10,130,1]{2,0,3,1:T(2,128)S(1)} %copy.344), channel_id=1, source_target_pairs={{0,1},{1,2},{2,3},{4,5},{5,6},{6,7},{8,9},{9,10},{10,11},{12,13},{... | collective-permute-start | bytes 31208 | tf_op jit(solution)/shard_map/ppermute | solution.py:28
  87.1 3.4 %copy-start.4 = (f32[8,128,128]{2,1,0:T(8,128)S(1)}, f32[8,128,128]{2,1,0:T(8,128)}, u32[]{:S(2)}) copy-start(f32[8,128,128]{2,1,0:T(8,128)} %param.7) | copy-start | bytes 1572868
  90.9 6.6 %copy-start.6 = (f32[24,48,50]{1,2,0:T(8,128)S(1)}, f32[24,48,50]{1,2,0:T(8,128)}, u32[]{:S(2)}) copy-start(f32[24,48,50]{1,2,0:T(8,128)} %copy.356) | copy-start | bytes 691204
  91.0 9.2 %collective-permute-start.12 = (f32[2,1,128,128]{3,2,1,0:T(8,128)S(1)}, f32[2,1,128,128]{3,2,1,0:T(8,128)S(1)}, u32[]{:S(2)}, u32[]{:S(2)}) collective-permute-start(f32[2,1,128,128]{3,2,1,0:T(8,128)S(1)} %get-tuple-element.35), channel_id=1, source_target_pairs={{16,0},{17,1},{18,2},{19,3},{20,4},{21,5},{22,6},{23,7},{24,8},{25... | collective-permute-start | bytes 393224 | tf_op jit(solution)/shard_map/ppermute | solution.py:29
  96.2 8.2 %collective-permute-start.13 = (f32[2,1,128,128]{3,2,1,0:T(8,128)S(1)}, f32[2,1,128,128]{3,2,1,0:T(8,128)S(1)}, u32[]{:S(2)}, u32[]{:S(2)}) collective-permute-start(f32[2,1,128,128]{3,2,1,0:T(8,128)S(1)} %get-tuple-element.34), channel_id=1, source_target_pairs={{0,16},{1,17},{2,18},{3,19},{4,20},{5,21},{6,22},{7,23},{8,24},{9,... | collective-permute-start | bytes 393224 | tf_op jit(solution)/shard_map/ppermute | solution.py:28
  104.4 4.7 %collective-permute-start.14 = (f32[2,10,1,128]{3,0,2,1:T(2,128)S(1)}, f32[2,10,1,128]{3,0,2,1:T(2,128)S(1)}, u32[]{:S(2)}, u32[]{:S(2)}) collective-permute-start(f32[2,10,1,128]{3,0,2,1:T(2,128)S(1)} %copy.346), channel_id=1, source_target_pairs={{4,0},{8,4},{12,8},{5,1},{9,5},{13,9},{6,2},{10,6},{14,10},{7,3},{... | collective-permute-start | bytes 30728 | tf_op jit(solution)/shard_map/ppermute | solution.py:29
  106.8 5.6 %collective-permute-start.15 = (f32[2,10,1,128]{3,0,2,1:T(2,128)S(1)}, f32[2,10,1,128]{3,0,2,1:T(2,128)S(1)}, u32[]{:S(2)}, u32[]{:S(2)}) collective-permute-start(f32[2,10,1,128]{3,0,2,1:T(2,128)S(1)} %copy.348), channel_id=1, source_target_pairs={{0,4},{4,8},{8,12},{1,5},{5,9},{9,13},{2,6},{6,10},{10,14},{3,7},{... | collective-permute-start | bytes 30728 | tf_op jit(solution)/shard_map/ppermute | solution.py:28
  109.2 57.0 %copy-start.1 = (f32[8,32,384]{2,1,0:T(8,128)}, f32[8,32,384]{2,1,0:T(8,128)S(1)}, u32[]{:S(2)}) copy-start(f32[8,32,384]{2,1,0:T(8,128)S(1)} %constant_dynamic-slice_fusion.2) | copy-start | bytes 1179652
  116.6 12.2 %collective-permute-start.16 = (f32[2,10,130,1]{2,0,3,1:T(2,128)S(1)}, f32[2,10,130,1]{2,0,3,1:T(2,128)S(1)}, u32[]{:S(2)}, u32[]{:S(2)}) collective-permute-start(f32[2,10,130,1]{2,0,3,1:T(2,128)S(1)} %copy.352), channel_id=1, source_target_pairs={{1,0},{2,1},{3,2},{5,4},{6,5},{7,6},{9,8},{10,9},{11,10},{13,12},{... | collective-permute-start | bytes 31208 | tf_op jit(solution)/shard_map/ppermute | solution.py:29
  120.0 10.4 %collective-permute-start.17 = (f32[2,10,130,1]{2,0,3,1:T(2,128)S(1)}, f32[2,10,130,1]{2,0,3,1:T(2,128)S(1)}, u32[]{:S(2)}, u32[]{:S(2)}) collective-permute-start(f32[2,10,130,1]{2,0,3,1:T(2,128)S(1)} %copy.354), channel_id=1, source_target_pairs={{0,1},{1,2},{2,3},{4,5},{5,6},{6,7},{8,9},{9,10},{10,11},{12,13},{... | collective-permute-start | bytes 31208 | tf_op jit(solution)/shard_map/ppermute | solution.py:28
  124.5 41.6 %collective-permute-start.20 = (f32[10,1,384]{2,1,0:T(1,128)}, f32[10,1,384]{2,1,0:T(1,128)S(1)}, u32[]{:S(2)}, u32[]{:S(2)}) collective-permute-start(f32[10,1,384]{2,1,0:T(1,128)} %get-tuple-element.48), channel_id=1, source_target_pairs={{1,0},{2,1},{3,2},{4,3},{5,4},{6,5},{7,6},{8,7},{9,8},{10,9},{11,1... | collective-permute-start | bytes 46088 | tf_op jit(solution)/shard_map/ppermute | solution.py:29
  126.4 39.7 %collective-permute-start.21 = (f32[10,1,384]{2,1,0:T(1,128)}, f32[10,1,384]{2,1,0:T(1,128)}, u32[]{:S(2)}, u32[]{:S(2)}) collective-permute-start(f32[10,1,384]{2,1,0:T(1,128)} %get-tuple-element.49), channel_id=1, source_target_pairs={{0,1},{1,2},{2,3},{3,4},{4,5},{5,6},{6,7},{7,8},{8,9},{9,10},{10,1... | collective-permute-start | bytes 46088 | tf_op jit(solution)/shard_map/ppermute | solution.py:28
  132.0 3.4 %copy-start.8 = (f32[128,128]{1,0:T(8,128)S(1)}, f32[128,128]{1,0:T(8,128)}, u32[]{:S(2)}) copy-start(f32[128,128]{1,0:T(8,128)} %copy-done.7) | copy-start | bytes 196612
  138.1 30.2 %all-to-all-start = ((f32[8,128,128]{2,0,1:T(8,128)}), f32[8,128,128]{2,0,1:T(8,128)}, u32[]{:S(2)}, u32[]{:S(2)}) async-start(f32[8,128,128]{2,0,1:T(8,128)} %copy.364), calls=%async_computation | async-start | bytes 1048576 | tf_op jit(solution)/shard_map/all_to_all | solution.py:148
  174.7 3.3 %collective-permute-start.22 = (f32[1,32,384]{2,1,0:T(8,128)S(1)}, f32[1,32,384]{2,1,0:T(8,128)S(1)}, u32[]{:S(2)}, u32[]{:S(2)}) collective-permute-start(f32[1,32,384]{2,1,0:T(8,128)S(1)} %get-tuple-element.55), channel_id=1, source_target_pairs={{16,0},{17,1},{18,2},{19,3},{20,4},{21,5},{22,6},{23,7},{24,8},{25... | collective-permute-start | bytes 147464 | tf_op jit(solution)/shard_map/ppermute | solution.py:29
  176.2 6.4 %collective-permute-start.23 = (f32[1,32,384]{2,1,0:T(8,128)S(1)}, f32[1,32,384]{2,1,0:T(8,128)S(1)}, u32[]{:S(2)}, u32[]{:S(2)}) collective-permute-start(f32[1,32,384]{2,1,0:T(8,128)S(1)} %get-tuple-element.54), channel_id=1, source_target_pairs={{0,16},{1,17},{2,18},{3,19},{4,20},{5,21},{6,22},{7,23},{8,24},{9,... | collective-permute-start | bytes 147464 | tf_op jit(solution)/shard_map/ppermute | solution.py:28
  182.6 4.7 %collective-permute-start.24 = (f32[10,1,384]{2,1,0:T(1,128)S(1)}, f32[10,1,384]{2,1,0:T(1,128)S(1)}, u32[]{:S(2)}, u32[]{:S(2)}) collective-permute-start(f32[10,1,384]{2,1,0:T(1,128)S(1)} %get-tuple-element.46), channel_id=1, source_target_pairs={{1,0},{2,1},{3,2},{4,3},{5,4},{6,5},{7,6},{8,7},{9,8},{10,9},{11,1... | collective-permute-start | bytes 46088 | tf_op jit(solution)/shard_map/ppermute | solution.py:29
  185.4 5.9 %collective-permute-start.25 = (f32[10,1,384]{2,1,0:T(1,128)S(1)}, f32[10,1,384]{2,1,0:T(1,128)S(1)}, u32[]{:S(2)}, u32[]{:S(2)}) collective-permute-start(f32[10,1,384]{2,1,0:T(1,128)S(1)} %get-tuple-element.47), channel_id=1, source_target_pairs={{0,1},{1,2},{2,3},{3,4},{4,5},{5,6},{6,7},{7,8},{8,9},{9,10},{10,1... | collective-permute-start | bytes 46088 | tf_op jit(solution)/shard_map/ppermute | solution.py:28
  192.6 3.4 %collective-permute-start.26 = (f32[1,32,384]{2,1,0:T(8,128)S(1)}, f32[1,32,384]{2,1,0:T(8,128)S(1)}, u32[]{:S(2)}, u32[]{:S(2)}) collective-permute-start(f32[1,32,384]{2,1,0:T(8,128)S(1)} %get-tuple-element.53), channel_id=1, source_target_pairs={{16,0},{17,1},{18,2},{19,3},{20,4},{21,5},{22,6},{23,7},{24,8},{25... | collective-permute-start | bytes 147464 | tf_op jit(solution)/shard_map/ppermute | solution.py:29
  194.3 6.0 %collective-permute-start.27 = (f32[1,32,384]{2,1,0:T(8,128)S(1)}, f32[1,32,384]{2,1,0:T(8,128)S(1)}, u32[]{:S(2)}, u32[]{:S(2)}) collective-permute-start(f32[1,32,384]{2,1,0:T(8,128)S(1)} %get-tuple-element.52), channel_id=1, source_target_pairs={{0,16},{1,17},{2,18},{3,19},{4,20},{5,21},{6,22},{7,23},{8,24},{9,... | collective-permute-start | bytes 147464 | tf_op jit(solution)/shard_map/ppermute | solution.py:28
  200.3 4.3 %collective-permute-start.28 = (f32[10,1,384]{2,1,0:T(1,128)S(1)}, f32[10,1,384]{2,1,0:T(1,128)S(1)}, u32[]{:S(2)}, u32[]{:S(2)}) collective-permute-start(f32[10,1,384]{2,1,0:T(1,128)S(1)} %get-tuple-element.44), channel_id=1, source_target_pairs={{1,0},{2,1},{3,2},{4,3},{5,4},{6,5},{7,6},{8,7},{9,8},{10,9},{11,1... | collective-permute-start | bytes 46088 | tf_op jit(solution)/shard_map/ppermute | solution.py:29
  202.2 5.9 %collective-permute-start.29 = (f32[10,1,384]{2,1,0:T(1,128)S(1)}, f32[10,1,384]{2,1,0:T(1,128)S(1)}, u32[]{:S(2)}, u32[]{:S(2)}) collective-permute-start(f32[10,1,384]{2,1,0:T(1,128)S(1)} %get-tuple-element.45), channel_id=1, source_target_pairs={{0,1},{1,2},{2,3},{3,4},{4,5},{5,6},{6,7},{7,8},{8,9},{9,10},{10,1... | collective-permute-start | bytes 46088 | tf_op jit(solution)/shard_map/ppermute | solution.py:28
  209.5 3.3 %collective-permute-start.30 = (f32[1,32,384]{2,1,0:T(8,128)S(1)}, f32[1,32,384]{2,1,0:T(8,128)S(1)}, u32[]{:S(2)}, u32[]{:S(2)}) collective-permute-start(f32[1,32,384]{2,1,0:T(8,128)S(1)} %get-tuple-element.51), channel_id=1, source_target_pairs={{16,0},{17,1},{18,2},{19,3},{20,4},{21,5},{22,6},{23,7},{24,8},{25... | collective-permute-start | bytes 147464 | tf_op jit(solution)/shard_map/ppermute | solution.py:29
  211.1 6.0 %collective-permute-start.31 = (f32[1,32,384]{2,1,0:T(8,128)S(1)}, f32[1,32,384]{2,1,0:T(8,128)S(1)}, u32[]{:S(2)}, u32[]{:S(2)}) collective-permute-start(f32[1,32,384]{2,1,0:T(8,128)S(1)} %get-tuple-element.50), channel_id=1, source_target_pairs={{0,16},{1,17},{2,18},{3,19},{4,20},{5,21},{6,22},{7,23},{8,24},{9,... | collective-permute-start | bytes 147464 | tf_op jit(solution)/shard_map/ppermute | solution.py:28
  217.1 4.3 %collective-permute-start.32 = (f32[10,1,384]{2,1,0:T(1,128)S(1)}, f32[10,1,384]{2,1,0:T(1,128)S(1)}, u32[]{:S(2)}, u32[]{:S(2)}) collective-permute-start(f32[10,1,384]{2,1,0:T(1,128)S(1)} %get-tuple-element.42), channel_id=1, source_target_pairs={{1,0},{2,1},{3,2},{4,3},{5,4},{6,5},{7,6},{8,7},{9,8},{10,9},{11,1... | collective-permute-start | bytes 46088 | tf_op jit(solution)/shard_map/ppermute | solution.py:29
  219.0 5.9 %collective-permute-start.33 = (f32[10,1,384]{2,1,0:T(1,128)S(1)}, f32[10,1,384]{2,1,0:T(1,128)S(1)}, u32[]{:S(2)}, u32[]{:S(2)}) collective-permute-start(f32[10,1,384]{2,1,0:T(1,128)S(1)} %get-tuple-element.43), channel_id=1, source_target_pairs={{0,1},{1,2},{2,3},{3,4},{4,5},{5,6},{6,7},{7,8},{8,9},{9,10},{10,1... | collective-permute-start | bytes 46088 | tf_op jit(solution)/shard_map/ppermute | solution.py:28
  227.0 11.4 %collective-permute-start.34 = (f32[8,32,384]{2,1,0:T(8,128)}, f32[8,32,384]{2,1,0:T(8,128)S(1)}, u32[]{:S(2)}, u32[]{:S(2)}) collective-permute-start(f32[8,32,384]{2,1,0:T(8,128)} %fusion.167), channel_id=1, source_target_pairs={{0,1},{1,2},{2,3},{3,0},{4,5},{5,6},{6,7},{7,4},{8,9},{9,10},{10,1... | collective-permute-start | bytes 1179656 | tf_op jit(solution)/shard_map/ppermute | solution.py:170
  227.0 13.7 %collective-permute-start.36 = (f32[8,32,384]{2,1,0:T(8,128)}, f32[8,32,384]{2,1,0:T(8,128)S(1)}, u32[]{:S(2)}, u32[]{:S(2)}) collective-permute-start(f32[8,32,384]{2,1,0:T(8,128)} %fusion.167), channel_id=1, source_target_pairs={{1,0},{2,1},{3,2},{0,3},{5,4},{6,5},{7,6},{4,7},{9,8},{10,9},{11,1... | collective-permute-start | bytes 1179656 | tf_op jit(solution)/shard_map/ppermute | solution.py:172
  238.4 7.2 %collective-permute-start.35 = (f32[8,32,384]{2,1,0:T(8,128)S(1)}, f32[8,32,384]{2,1,0:T(8,128)S(1)}, u32[]{:S(2)}, u32[]{:S(2)}) collective-permute-start(f32[8,32,384]{2,1,0:T(8,128)S(1)} %collective-permute-done.34), channel_id=1, source_target_pairs={{0,1},{1,2},{2,3},{3,0},{4,5},{5,6},{6,7},{7,4},{8,9},{9,10},{10,1... | collective-permute-start | bytes 1179656 | tf_op jit(solution)/shard_map/ppermute | solution.py:170
  (3 other events, 5.5 us)
